TPU v7x, 512 devices: a whole 4x4x16 slice. The times are simulated.
512 devices in a mesh: seq: 64 (over z, y), tp: 4 (over x), dp: 2 (over core).
Axes of the slice: x: 4, y: 4, z: 16, core: 2. Of those that a mesh axis runs over, the one named last changes fastest.
Arguments:
- inputs: bfloat16 [16384, 1280], P(('dp', 'seq'), 'tp'), parts along dimension 0, may hold values from -6 to 6
- out_grads: bfloat16 [16384, 1280], P(('dp', 'seq'), 'tp'), parts along dimension 0, may hold values from -6 to 6
- norm_gain: float32 [1280], replicated, may hold values from 0.1 to 1.9
- w_query: bfloat16 [640, 1280], P('tp'), may hold values from -0.15625 to 0.15625
- w_key: bfloat16 [640, 1280], P('tp'), may hold values from -0.15625 to 0.15625
- w_value: bfloat16 [640, 1280], P('tp'), may hold values from -0.15625 to 0.15625
- w_output: bfloat16 [640, 1280], P('tp'), may hold values from -0.25 to 0.25
- query_scale: float32 [80], replicated, may hold values from -4 to 4
- offsets: int32 [64], replicated, may hold values from 0 to 63, each once
Outputs:
- input_grads: bfloat16 [16384, 1280], P(('dp', 'seq'), 'tp'), parts along dimension 0
There are 2 independent parts, one for each index of `dp`. A program takes and returns all parts, laid end to end along the dimension named above; an argument that names none is the same for every part. Nothing has to cross between parts.
Inputs may be any that keep to these rules, and one draw needn't show every extreme that they name: `offsets`: each number appears exactly once.
All inputs are finite; a program needn't handle non-finite values.
Results may differ from a plain program's by a relative error of at most 0.007.
The roundings to bfloat16 on the way count: a program that leaves them out, or rounds other values in their place, can miss the bound.
Values may be sent and summed in bfloat16 or wider, within the bound.
No kernel may reach another device: no remote copies, remote signals or barrier semaphores. Data moves between devices by JAX's collectives and lax.ppermute only.
A program may use at most 64 MiB of HBM per device.

v0:
```python
import math
import jax
import jax.numpy as jnp
import numpy as np
from jax import lax
from jax.sharding import Mesh
from jax.sharding import PartitionSpec as P

PIECE = 128
scale_base = 1.4426950408889634
masked_score = -1e30
norm_eps = 1e-06


def column_scale(query_scale, head_count):
    head_width = query_scale.shape[0]
    factor = scale_base / math.sqrt(head_width) * jax.nn.softplus(query_scale)
    return jnp.tile(factor, head_count)


def block_positions(offsets, rows):
    return (offsets[:, None] * PIECE + lax.iota(jnp.int32, PIECE)[None, :]).reshape(rows)


def ring_steps(size):
    return (size // 2, (size - 1) // 2)


def shift(data, axis, size, step):
    return lax.ppermute(data, axis, [(i, (i + step) % size) for i in range(size)])


def ring_gather(data, axis, size):
    forward, backward = ring_steps(size)
    pieces = [None] * size
    pieces[0] = data
    ahead = behind = data
    for step in range(max(forward, backward)):
        if step < forward:
            ahead = shift(ahead, axis, size, 1)
            pieces[size - 1 - step] = ahead
        if step < backward:
            behind = shift(behind, axis, size, -1)
            pieces[1 + step] = behind
    return pieces


def ring4_first(data, axis):
    return (shift(data, axis, 4, 1), shift(data, axis, 4, -1))


def ring4_last(data, ahead, behind, axis):
    half = data.shape[0] // 2
    far = jnp.concatenate(
        [shift(ahead[:half], axis, 4, 1), shift(behind[half:], axis, 4, -1)], axis=0
    )
    return [data, behind, far, ahead]


def per_device(
    inputs, out_grads, norm_gain, w_query, w_key, w_value, w_output, query_scale, offsets
):
    row_count, width_here = inputs.shape
    head_width = query_scale.shape[0]
    heads_here = w_query.shape[0] // head_width
    cols = heads_here * head_width
    tp_size = lax.axis_size("tp")
    y_size = lax.axis_size("y")
    shards = offsets.shape[0]
    all_rows = shards * row_count
    contract = (((1,), (1,)), ((), ()))
    with jax.named_scope("gather_features"):
        both = jnp.concatenate([inputs, out_grads], axis=1)
        gathered = lax.all_gather(both, "tp", axis=1, tiled=True)
        gathered = gathered.reshape(row_count, tp_size, 2, width_here)
        full_inputs = gathered[:, :, 0, :].reshape(row_count, tp_size * width_here)
        full_grads = gathered[:, :, 1, :].reshape(row_count, tp_size * width_here)
    full_width = full_inputs.shape[1]
    with jax.named_scope("projections"):
        widened = full_inputs.astype(jnp.float32)
        inverse = lax.rsqrt(jnp.mean(widened * widened, axis=1, keepdims=True) + norm_eps)
        normed = (widened * inverse * norm_gain[None, :]).astype(jnp.bfloat16)
        factor = column_scale(query_scale, heads_here)
        queries = (
            lax.dot_general(normed, w_query, contract, preferred_element_type=jnp.float32)
            * factor[None, :]
        ).astype(jnp.bfloat16)
        keys = lax.dot_general(normed, w_key, contract, preferred_element_type=jnp.float32).astype(
            jnp.bfloat16
        )
        values = lax.dot_general(
            normed, w_value, contract, preferred_element_type=jnp.float32
        ).astype(jnp.bfloat16)
        head_grads = lax.dot_general(
            full_grads, w_output, contract, preferred_element_type=jnp.float32
        ).astype(jnp.bfloat16)
    z_size = lax.axis_size("z")
    z_index = lax.axis_index("z")
    y_index = lax.axis_index("y")
    with jax.named_scope("gather_sequence"):
        kv = jnp.concatenate([keys, values], axis=1)
        qg = jnp.concatenate([queries, head_grads], axis=1)
        kv_all = lax.all_gather(kv, "y", axis=0, tiled=True)
        kv_all = lax.all_gather(kv_all, "z", axis=0, tiled=True)
        qg_z = jnp.concatenate(ring_gather(qg, "z", z_size), axis=0)
        qg_ahead, qg_behind = ring4_first(qg_z, "y")
        key_all = kv_all[:, :cols].reshape(all_rows, heads_here, head_width)
        value_all = kv_all[:, cols:].reshape(all_rows, heads_here, head_width)
    rel_z = lax.iota(jnp.int32, z_size)
    rel_y = lax.iota(jnp.int32, y_size)
    abs_z = (z_index + rel_z) % z_size
    abs_y = (y_index + rel_y) % y_size
    qg_source = (abs_z[None, :] * y_size + abs_y[:, None]).reshape(shards)
    key_positions = block_positions(offsets, all_rows)
    seq_index = z_index * y_size + y_index
    own_positions = offsets[seq_index] * PIECE + lax.iota(jnp.int32, row_count)
    query_heads = queries.reshape(row_count, heads_here, head_width)
    grad_heads = head_grads.reshape(row_count, heads_here, head_width)
    key_heads = keys.reshape(row_count, heads_here, head_width)
    value_heads = values.reshape(row_count, heads_here, head_width)
    with jax.named_scope("query_pass"):
        scores = jnp.einsum(
            "qhd,khd->hqk", query_heads, key_all, preferred_element_type=jnp.float32
        )
        visible = key_positions[None, None, :] <= own_positions[None, :, None]
        masked = jnp.where(visible, scores, masked_score)
        row_peak = jnp.max(masked, axis=2)
        summed = jnp.sum(jnp.where(visible, jnp.exp(masked - row_peak[:, :, None]), 0.0), axis=2)
        log_total = row_peak + jnp.log(summed)
        attend = jnp.exp(jnp.where(visible, scores - log_total[:, :, None], masked_score))
        grad_probs = jnp.einsum(
            "qhd,khd->hqk", grad_heads, value_all, preferred_element_type=jnp.float32
        )
        weighted = attend * grad_probs
        row_delta = jnp.sum(weighted, axis=2)
        first_sum = jnp.einsum(
            "hqk,khd->hqd",
            weighted.astype(jnp.bfloat16),
            key_all,
            preferred_element_type=jnp.float32,
        )
        second_sum = jnp.einsum(
            "hqk,khd->hqd", attend.astype(jnp.bfloat16), key_all, preferred_element_type=jnp.float32
        )
        query_grad = first_sum - row_delta[:, :, None] * second_sum
        query_grad = jnp.transpose(query_grad, (1, 0, 2)).reshape(row_count, cols)
        query_done = (query_grad * factor[None, :]).astype(jnp.bfloat16)
    with jax.named_scope("gather_row_stats"):
        stats = jnp.stack([log_total, row_delta], axis=0)
        stats, qg_ahead, qg_behind = lax.optimization_barrier((stats, qg_ahead, qg_behind))
        qg_pieces = ring4_last(qg_z, qg_ahead, qg_behind, "y")
        sent = jnp.broadcast_to(stats[None], (shards,) + stats.shape)
        stats_all = lax.all_to_all(sent, ("z", "y"), 0, 0, tiled=False)
    with jax.named_scope("key_pass"):
        piece_rows = qg_pieces[0].shape[0]
        stats_ordered = stats_all[qg_source]
        query_places = block_positions(offsets[qg_source], all_rows)
        key_grad = jnp.zeros((row_count, heads_here, head_width), jnp.float32)
        value_grad = jnp.zeros((row_count, heads_here, head_width), jnp.float32)
        for ry, piece in enumerate(qg_pieces):
            source = qg_source[ry * z_size : (ry + 1) * z_size]
            query_part = piece[:, :cols].reshape(piece_rows, heads_here, head_width)
            grad_part = piece[:, cols:].reshape(piece_rows, heads_here, head_width)
            place = query_places[ry * piece_rows : (ry + 1) * piece_rows]
            part_stats = stats_ordered[ry * z_size : (ry + 1) * z_size]
            log_part = jnp.transpose(part_stats[:, 0], (1, 0, 2)).reshape(heads_here, piece_rows)
            delta_part = jnp.transpose(part_stats[:, 1], (1, 0, 2)).reshape(heads_here, piece_rows)
            scores_t = jnp.einsum(
                "khd,qhd->hkq", key_heads, query_part, preferred_element_type=jnp.float32
            )
            visible_t = own_positions[None, :, None] <= place[None, None, :]
            attend_t = jnp.exp(jnp.where(visible_t, scores_t - log_part[:, None, :], masked_score))
            grad_probs_t = jnp.einsum(
                "khd,qhd->hkq", value_heads, grad_part, preferred_element_type=jnp.float32
            )
            score_grad = (attend_t * (grad_probs_t - delta_part[:, None, :])).astype(jnp.bfloat16)
            plain_t = attend_t.astype(jnp.bfloat16)
            score_grad, plain_t = lax.optimization_barrier((score_grad, plain_t))
            key_grad = key_grad + jnp.einsum(
                "hkq,qhd->khd", score_grad, query_part, preferred_element_type=jnp.float32
            )
            value_grad = value_grad + jnp.einsum(
                "hkq,qhd->khd", plain_t, grad_part, preferred_element_type=jnp.float32
            )
        key_done = key_grad.reshape(row_count, cols).astype(jnp.bfloat16)
        value_done = value_grad.reshape(row_count, cols).astype(jnp.bfloat16)
    with jax.named_scope("back_projection"):
        back_sum = jnp.dot(query_done, w_query, preferred_element_type=jnp.float32)
        back_sum = back_sum + jnp.dot(key_done, w_key, preferred_element_type=jnp.float32)
        back_sum = back_sum + jnp.dot(value_done, w_value, preferred_element_type=jnp.float32)
        scaled = back_sum * norm_gain[None, :]
        row_part = jnp.sum(widened * scaled, axis=1)
        chunks = scaled.reshape(row_count, tp_size, width_here).transpose(1, 0, 2)
        extra = jnp.zeros((tp_size, 1, width_here), jnp.float32)
        extra = extra.at[:, 0, :row_count].set(jnp.broadcast_to(row_part, (tp_size, row_count)))
        payload = jnp.concatenate([chunks, extra], axis=1)
        received = lax.all_to_all(payload, "tp", 0, 0, tiled=False)
        total = jnp.sum(received, axis=0)
        scaled_own = total[:row_count]
        row_dot = total[row_count, :row_count][:, None]
    with jax.named_scope("input_grads"):
        start_col = lax.axis_index("tp") * width_here
        own_inputs = inputs.astype(jnp.float32)
        branch = (
            inverse * scaled_own - own_inputs * inverse * inverse * inverse * row_dot / full_width
        )
        result = out_grads.astype(jnp.float32) + branch
    return result.astype(jnp.bfloat16)


def solution(mesh):
    seq_size = mesh.shape["seq"]
    devices = mesh.devices
    y_size = 4 if seq_size % 4 == 0 else 1
    split = Mesh(
        devices.reshape((seq_size // y_size, y_size) + devices.shape[1:]), ("z", "y", "tp", "dp")
    )
    rows = P(("dp", "z", "y"), "tp")
    return jax.shard_map(
        per_device,
        mesh=split,
        in_specs=(
            rows,
            rows,
            P(),
            P("tp", None),
            P("tp", None),
            P("tp", None),
            P("tp", None),
            P(),
            P(),
        ),
        out_specs=rows,
        check_vma=False,
    )
```

profile of v0, /device:TPU:2, one launch (start us, length us, event | category | flops | bytes accessed | tf_op | source)
XLA Modules:
  0.0 219.6 jit_solution(6411096085846394718)
XLA Ops:
  7.5 15.7 %all_gather.9 = bf16[128,2560]{0,1:T(8,128)(2,1)S(1)} all-gather(bf16[128,640]{0,1:T(8,128)(2,1)S(1)} %pad_maximum_fusion.1), channel_id=1, replica_groups=mesh['z'=16,'y'=4,'tp'=4,'dp'=2] {'tp'}, dimensions={1}, use_global_device_ids=true | all-gather | bytes 819200 | tf_op jit(solution)/shard_map/gather_features/all_gather | solution.py:74
  24.7 12.3 %all_gather.10 = bf16[512,320]{0,1:T(8,128)(2,1)} all-gather(bf16[128,320]{0,1:T(8,128)(2,1)S(1)} %pad_maximum_fusion.2), channel_id=1, replica_groups=mesh['z'=16,'y'=4,'tp'=4,'dp'=2] {'y'}, dimensions={0}, use_global_device_ids=true | all-gather | bytes 409600 | tf_op jit(solution)/shard_map/gather_sequence/all_gather | solution.py:103
  38.4 10.8 %collective-permute-start = (bf16[128,320]{0,1:T(8,128)(2,1)S(1)}, bf16[128,320]{0,1:T(8,128)(2,1)S(1)}, u32[]{:S(2)}, u32[]{:S(2)}) collective-permute-start(bf16[128,320]{0,1:T(8,128)(2,1)S(1)} %get-tuple-element.59), channel_id=1, source_target_pairs={{0,480},{32,0},{64,32},{96,64},{128,96},{160,128},{192,160},{224,1... | collective-permute-start | bytes 245768 | tf_op jit(solution)/shard_map/gather_sequence/ppermute | solution.py:30
  55.8 5.1 %collective-permute-start.1 = (bf16[128,320]{0,1:T(8,128)(2,1)S(1)}, bf16[128,320]{0,1:T(8,128)(2,1)S(1)}, u32[]{:S(2)}, u32[]{:S(2)}) collective-permute-start(bf16[128,320]{0,1:T(8,128)(2,1)S(1)} %collective-permute-done), channel_id=1, source_target_pairs={{0,480},{32,0},{64,32},{96,64},{128,96},{160,128},{192,160},{224,1... | collective-permute-start | bytes 245768 | tf_op jit(solution)/shard_map/gather_sequence/ppermute | solution.py:30
  64.5 5.6 %collective-permute-start.2 = (bf16[128,320]{0,1:T(8,128)(2,1)S(1)}, bf16[128,320]{0,1:T(8,128)(2,1)S(1)}, u32[]{:S(2)}, u32[]{:S(2)}) collective-permute-start(bf16[128,320]{0,1:T(8,128)(2,1)S(1)} %collective-permute-done.1), channel_id=1, source_target_pairs={{0,480},{32,0},{64,32},{96,64},{128,96},{160,128},{192,160},{224,1... | collective-permute-start | bytes 245768 | tf_op jit(solution)/shard_map/gather_sequence/ppermute | solution.py:30
  73.3 5.6 %collective-permute-start.3 = (bf16[128,320]{0,1:T(8,128)(2,1)S(1)}, bf16[128,320]{0,1:T(8,128)(2,1)S(1)}, u32[]{:S(2)}, u32[]{:S(2)}) collective-permute-start(bf16[128,320]{0,1:T(8,128)(2,1)S(1)} %collective-permute-done.2), channel_id=1, source_target_pairs={{0,480},{32,0},{64,32},{96,64},{128,96},{160,128},{192,160},{224,1... | collective-permute-start | bytes 245768 | tf_op jit(solution)/shard_map/gather_sequence/ppermute | solution.py:30
  82.7 5.6 %collective-permute-start.4 = (bf16[128,320]{0,1:T(8,128)(2,1)S(1)}, bf16[128,320]{0,1:T(8,128)(2,1)S(1)}, u32[]{:S(2)}, u32[]{:S(2)}) collective-permute-start(bf16[128,320]{0,1:T(8,128)(2,1)S(1)} %collective-permute-done.3), channel_id=1, source_target_pairs={{0,480},{32,0},{64,32},{96,64},{128,96},{160,128},{192,160},{224,1... | collective-permute-start | bytes 245768 | tf_op jit(solution)/shard_map/gather_sequence/ppermute | solution.py:30
  91.5 5.6 %collective-permute-start.5 = (bf16[128,320]{0,1:T(8,128)(2,1)S(1)}, bf16[128,320]{0,1:T(8,128)(2,1)S(1)}, u32[]{:S(2)}, u32[]{:S(2)}) collective-permute-start(bf16[128,320]{0,1:T(8,128)(2,1)S(1)} %collective-permute-done.4), channel_id=1, source_target_pairs={{0,480},{32,0},{64,32},{96,64},{128,96},{160,128},{192,160},{224,1... | collective-permute-start | bytes 245768 | tf_op jit(solution)/shard_map/gather_sequence/ppermute | solution.py:30
  100.4 5.6 %collective-permute-start.6 = (bf16[128,320]{0,1:T(8,128)(2,1)S(1)}, bf16[128,320]{0,1:T(8,128)(2,1)S(1)}, u32[]{:S(2)}, u32[]{:S(2)}) collective-permute-start(bf16[128,320]{0,1:T(8,128)(2,1)S(1)} %collective-permute-done.5), channel_id=1, source_target_pairs={{0,480},{32,0},{64,32},{96,64},{128,96},{160,128},{192,160},{224,1... | collective-permute-start | bytes 245768 | tf_op jit(solution)/shard_map/gather_sequence/ppermute | solution.py:30
  109.3 6.3 %collective-permute-done.13 = bf16[128,320]{0,1:T(8,128)(2,1)S(1)} collective-permute-done((bf16[128,320]{0,1:T(8,128)(2,1)S(1)}, bf16[128,320]{0,1:T(8,128)(2,1)S(1)}, u32[]{:S(2)}, u32[]{:S(2)}) %collective-permute-start.13) | collective-permute-done | bytes 81952 | tf_op jit(solution)/shard_map/gather_sequence/ppermute | solution.py:30
  118.1 6.3 %collective-permute-done.14 = bf16[128,320]{0,1:T(8,128)(2,1)S(1)} collective-permute-done((bf16[128,320]{0,1:T(8,128)(2,1)S(1)}, bf16[128,320]{0,1:T(8,128)(2,1)S(1)}, u32[]{:S(2)}, u32[]{:S(2)}) %collective-permute-start.14) | collective-permute-done | bytes 81952 | tf_op jit(solution)/shard_map/gather_sequence/ppermute | solution.py:30
  129.6 3.5 %collective-permute-start.15 = (bf16[2048,320]{0,1:T(8,128)(2,1)}, bf16[2048,320]{0,1:T(8,128)(2,1)}, u32[]{:S(2)}, u32[]{:S(2)}) collective-permute-start(bf16[2048,320]{0,1:T(8,128)(2,1)} %constant_dynamic-update-slice_fusion), channel_id=1, source_target_pairs={{0,8},{8,16},{16,24},{24,0},{1,9},{9,17},{17,25},{25,1},{2,10},{10... | collective-permute-start | bytes 3932168 | tf_op jit(solution)/shard_map/gather_sequence/ppermute | solution.py:30
  133.2 3.7 %collective-permute-start.16 = (bf16[2048,320]{0,1:T(8,128)(2,1)}, bf16[2048,320]{0,1:T(8,128)(2,1)}, u32[]{:S(2)}, u32[]{:S(2)}) collective-permute-start(bf16[2048,320]{0,1:T(8,128)(2,1)} %constant_dynamic-update-slice_fusion), channel_id=1, source_target_pairs={{0,24},{8,0},{16,8},{24,16},{1,25},{9,1},{17,9},{25,17},{2,26},{10... | collective-permute-start | bytes 3932168 | tf_op jit(solution)/shard_map/gather_sequence/ppermute | solution.py:30
  136.9 2.2 %fusion.52 = (bf16[2048,160]{0,1:T(8,128)(2,1)}, bf16[2048,160]{0,1:T(8,128)(2,1)S(1)}) fusion(bf16[2048,320]{0,1:T(8,128)(2,1)} %constant_dynamic-update-slice_fusion), kind=kLoop, calls=%fused_computation.129 | loop fusion | bytes 2621440 | tf_op jit(solution)/shard_map/key_pass/slice | solution.py:163
  139.1 3.0 %fusion.51 = (bf16[8192,160]{0,1:T(8,128)(2,1)S(1)}, bf16[8192,160]{0,1:T(8,128)(2,1)S(1)}) fusion(bf16[8192,320]{0,1:T(8,128)(2,1)} %all-gather.2.cloned.1.call-done), kind=kLoop, calls=%fused_computation.128 | loop fusion | bytes 10485760 | tf_op jit(solution)/shard_map/gather_sequence/slice | solution.py:108
  143.9 2.5 %select_reduce_fusion = f32[2,128]{1,0:T(2,128)S(1)} fusion(f32[2,128,8192]{2,1,0:T(8,128)S(1)} %get-tuple-element.70, f32[2,128]{1,0:T(2,128)S(1)} %get-tuple-element.69, pred[128,8192]{1,0:T(8,128)(4,1)S(1)} %broadcast_compare_fusion), kind=kLoop, calls=%fused_computation.4 | loop fusion | flops 8388352 | bytes 9439232 | tf_op jit(solution)/shard_map/query_pass/reduce_sum | solution.py:128
  146.4 3.5 %fusion.57 = (f32[2,128]{1,0:T(2,128)S(1)}, bf16[2,128,8192]{2,1,0:T(8,128)(2,1)S(1)}) fusion(bf16[128,2,80]{0,2,1:T(8,128)(2,1)S(1)} %bitcast.192, bf16[8192,2,80]{0,2,1:T(8,128)(2,1)S(1)} %bitcast.178, f32[2,128,8192]{2,1,0:T(8,128)S(1)} %get-tuple-element.70, f32[2,128]{1,0:T(2,128)S(1)} %log_add_fusion, pred[128,8192]{1,0:T(8,128)(4,1)S(1)} %broadcast_compare_fusion), kind=kOutput, calls=%fused_computation.134 | convolution fusion | flops 346029824 | bytes 16295936 | tf_op jit(solution)/shard_map/query_pass/qhd,khd->hqk/dot_general | solution.py:131
  155.3 8.6 %all-to-all-start = ((f32[64,2,2,128]{3,2,1,0:T(2,128)}), f32[64,2,2,128]{3,2,1,0:T(2,128)}, u32[]{:S(2)}, u32[]{:S(2)}) async-start(f32[64,2,2,128]{3,2,1,0:T(2,128)} %broadcast_in_dim.87), calls=%async_computation | async-start | bytes 262144 | tf_op jit(solution)/shard_map/gather_row_stats/all_to_all | solution.py:153
  164.0 2.0 slice.137
  166.0 3.4 %collective-permute-start.17 = (bf16[1024,320]{0,1:T(8,128)(2,1)}, bf16[1024,320]{0,1:T(8,128)(2,1)}, u32[]{:S(2)}, u32[]{:S(2)}) collective-permute-start(bf16[1024,320]{0,1:T(8,128)(2,1)} %slice.137), channel_id=1, source_target_pairs={{0,8},{8,16},{16,24},{24,0},{1,9},{9,17},{17,25},{25,1},{2,10},{10... | collective-permute-start | bytes 1966088 | tf_op jit(solution)/shard_map/gather_row_stats/ppermute | solution.py:30
  171.4 3.9 %collective-permute-start.18 = (bf16[1024,320]{0,1:T(8,128)(2,1)}, bf16[1024,320]{0,1:T(8,128)(2,1)}, u32[]{:S(2)}, u32[]{:S(2)}) collective-permute-start(bf16[1024,320]{0,1:T(8,128)(2,1)} %slice.138), channel_id=1, source_target_pairs={{0,24},{8,0},{16,8},{24,16},{1,25},{9,1},{17,9},{25,17},{2,26},{10... | collective-permute-start | bytes 1966088 | tf_op jit(solution)/shard_map/gather_row_stats/ppermute | solution.py:30
  175.3 3.0 %fusion.53 = (bf16[2048,160]{0,1:T(8,128)(2,1)}, bf16[2048,160]{0,1:T(8,128)(2,1)S(1)}, bf16[2048,160]{0,1:T(8,128)(2,1)S(1)}, bf16[2048,160]{0,1:T(8,128)(2,1)}) fusion(bf16[2048,320]{0,1:T(8,128)(2,1)} %collective-permute-done.16, bf16[2048,320]{0,1:T(8,128)(2,1)} %collective-permute-done.15), kind=kLoop, calls=%fused_computation.130 | loop fusion | bytes 5242880 | tf_op jit(solution)/shard_map/key_pass/slice | solution.py:163
  180.0 2.3 %gather_fusion.1 = f32[64,2,2,128]{3,2,1,0:T(2,128)} fusion(f32[64,2,2,128]{3,2,1,0:T(2,128)} %all-to-all-done, s32[1024]{0:T(1024)S(1)} %pad_clamp_fusion), kind=kCustom, calls=%fused_computation.1 | custom fusion | bytes 262400 | tf_op jit(solution)/shard_map/key_pass/gather | solution.py:156
  198.0 13.8 %all_to_all.10 = f32[4,129,320]{2,1,0:T(8,128)S(1)} all-to-all(f32[4,129,320]{2,1,0:T(8,128)S(1)} %copy.31), channel_id=1, replica_groups=mesh['z'=16,'y'=4,'tp'=4,'dp'=2] {'tp'}, dimensions={0} | all-to-all | bytes 1320960 | tf_op jit(solution)/shard_map/back_projection/all_to_all | solution.py:197
  (150 shorter events, 64.9 us)
Async XLA Ops:
  6.5 17.4 %copy-start = (bf16[160,1280]{1,0:T(8,128)(2,1)S(1)}, bf16[160,1280]{1,0:T(8,128)(2,1)}, u32[]{:S(2)}) copy-start(bf16[160,1280]{1,0:T(8,128)(2,1)} %param.16) | copy-start | bytes 1228804
  6.5 132.6 %all-gather.2.cloned.1.call-start = ((), (), s32[]{:S(2)}) async-start(), calls=%async_computation.2 | async-start | bytes 5570560 | tf_op jit(solution)/shard_map/gather_sequence/all_gather | solution.py:104
  7.5 16.3 %copy-start.15 = (f32[1280]{0:T(1024)S(1)}, f32[1280]{0:T(1024)}, u32[]{:S(2)}) copy-start(f32[1280]{0:T(1024)} %param.13) | copy-start | bytes 15364
  24.0 27.3 %copy-start.1 = (s32[64]{0:T(128)S(1)}, s32[64]{0:T(128)}, u32[]{:S(2)}) copy-start(s32[64]{0:T(128)} %param.19) | copy-start | bytes 772
  38.4 17.4 %collective-permute-start = (bf16[128,320]{0,1:T(8,128)(2,1)S(1)}, bf16[128,320]{0,1:T(8,128)(2,1)S(1)}, u32[]{:S(2)}, u32[]{:S(2)}) collective-permute-start(bf16[128,320]{0,1:T(8,128)(2,1)S(1)} %get-tuple-element.59), channel_id=1, source_target_pairs={{0,480},{32,0},{64,32},{96,64},{128,96},{160,128},{192,160},{224,1... | collective-permute-start | bytes 245768 | tf_op jit(solution)/shard_map/gather_sequence/ppermute | solution.py:30
  49.1 11.7 %collective-permute-start.7 = (bf16[128,320]{0,1:T(8,128)(2,1)S(1)}, bf16[128,320]{0,1:T(8,128)(2,1)S(1)}, u32[]{:S(2)}, u32[]{:S(2)}) collective-permute-start(bf16[128,320]{0,1:T(8,128)(2,1)S(1)} %get-tuple-element.59), channel_id=1, source_target_pairs={{0,32},{32,64},{64,96},{96,128},{128,160},{160,192},{192,224},{224... | collective-permute-start | bytes 245768 | tf_op jit(solution)/shard_map/gather_sequence/ppermute | solution.py:30
  55.8 8.7 %collective-permute-start.1 = (bf16[128,320]{0,1:T(8,128)(2,1)S(1)}, bf16[128,320]{0,1:T(8,128)(2,1)S(1)}, u32[]{:S(2)}, u32[]{:S(2)}) collective-permute-start(bf16[128,320]{0,1:T(8,128)(2,1)S(1)} %collective-permute-done), channel_id=1, source_target_pairs={{0,480},{32,0},{64,32},{96,64},{128,96},{160,128},{192,160},{224,1... | collective-permute-start | bytes 245768 | tf_op jit(solution)/shard_map/gather_sequence/ppermute | solution.py:30
  60.9 9.6 %collective-permute-start.8 = (bf16[128,320]{0,1:T(8,128)(2,1)S(1)}, bf16[128,320]{0,1:T(8,128)(2,1)S(1)}, u32[]{:S(2)}, u32[]{:S(2)}) collective-permute-start(bf16[128,320]{0,1:T(8,128)(2,1)S(1)} %collective-permute-done.7), channel_id=1, source_target_pairs={{0,32},{32,64},{64,96},{96,128},{128,160},{160,192},{192,224},{224... | collective-permute-start | bytes 245768 | tf_op jit(solution)/shard_map/gather_sequence/ppermute | solution.py:30
  64.5 8.9 %collective-permute-start.2 = (bf16[128,320]{0,1:T(8,128)(2,1)S(1)}, bf16[128,320]{0,1:T(8,128)(2,1)S(1)}, u32[]{:S(2)}, u32[]{:S(2)}) collective-permute-start(bf16[128,320]{0,1:T(8,128)(2,1)S(1)} %collective-permute-done.1), channel_id=1, source_target_pairs={{0,480},{32,0},{64,32},{96,64},{128,96},{160,128},{192,160},{224,1... | collective-permute-start | bytes 245768 | tf_op jit(solution)/shard_map/gather_sequence/ppermute | solution.py:30
  70.5 9.2 %collective-permute-start.9 = (bf16[128,320]{0,1:T(8,128)(2,1)S(1)}, bf16[128,320]{0,1:T(8,128)(2,1)S(1)}, u32[]{:S(2)}, u32[]{:S(2)}) collective-permute-start(bf16[128,320]{0,1:T(8,128)(2,1)S(1)} %collective-permute-done.8), channel_id=1, source_target_pairs={{0,32},{32,64},{64,96},{96,128},{128,160},{160,192},{192,224},{224... | collective-permute-start | bytes 245768 | tf_op jit(solution)/shard_map/gather_sequence/ppermute | solution.py:30
  73.3 9.3 %collective-permute-start.3 = (bf16[128,320]{0,1:T(8,128)(2,1)S(1)}, bf16[128,320]{0,1:T(8,128)(2,1)S(1)}, u32[]{:S(2)}, u32[]{:S(2)}) collective-permute-start(bf16[128,320]{0,1:T(8,128)(2,1)S(1)} %collective-permute-done.2), channel_id=1, source_target_pairs={{0,480},{32,0},{64,32},{96,64},{128,96},{160,128},{192,160},{224,1... | collective-permute-start | bytes 245768 | tf_op jit(solution)/shard_map/gather_sequence/ppermute | solution.py:30
  79.7 9.1 %collective-permute-start.10 = (bf16[128,320]{0,1:T(8,128)(2,1)S(1)}, bf16[128,320]{0,1:T(8,128)(2,1)S(1)}, u32[]{:S(2)}, u32[]{:S(2)}) collective-permute-start(bf16[128,320]{0,1:T(8,128)(2,1)S(1)} %collective-permute-done.9), channel_id=1, source_target_pairs={{0,32},{32,64},{64,96},{96,128},{128,160},{160,192},{192,224},{224... | collective-permute-start | bytes 245768 | tf_op jit(solution)/shard_map/gather_sequence/ppermute | solution.py:30
  82.7 8.9 %collective-permute-start.4 = (bf16[128,320]{0,1:T(8,128)(2,1)S(1)}, bf16[128,320]{0,1:T(8,128)(2,1)S(1)}, u32[]{:S(2)}, u32[]{:S(2)}) collective-permute-start(bf16[128,320]{0,1:T(8,128)(2,1)S(1)} %collective-permute-done.3), channel_id=1, source_target_pairs={{0,480},{32,0},{64,32},{96,64},{128,96},{160,128},{192,160},{224,1... | collective-permute-start | bytes 245768 | tf_op jit(solution)/shard_map/gather_sequence/ppermute | solution.py:30
  88.9 9.0 %collective-permute-start.11 = (bf16[128,320]{0,1:T(8,128)(2,1)S(1)}, bf16[128,320]{0,1:T(8,128)(2,1)S(1)}, u32[]{:S(2)}, u32[]{:S(2)}) collective-permute-start(bf16[128,320]{0,1:T(8,128)(2,1)S(1)} %collective-permute-done.10), channel_id=1, source_target_pairs={{0,32},{32,64},{64,96},{96,128},{128,160},{160,192},{192,224},{224... | collective-permute-start | bytes 245768 | tf_op jit(solution)/shard_map/gather_sequence/ppermute | solution.py:30
  91.5 8.9 %collective-permute-start.5 = (bf16[128,320]{0,1:T(8,128)(2,1)S(1)}, bf16[128,320]{0,1:T(8,128)(2,1)S(1)}, u32[]{:S(2)}, u32[]{:S(2)}) collective-permute-start(bf16[128,320]{0,1:T(8,128)(2,1)S(1)} %collective-permute-done.4), channel_id=1, source_target_pairs={{0,480},{32,0},{64,32},{96,64},{128,96},{160,128},{192,160},{224,1... | collective-permute-start | bytes 245768 | tf_op jit(solution)/shard_map/gather_sequence/ppermute | solution.py:30
  97.8 8.9 %collective-permute-start.12 = (bf16[128,320]{0,1:T(8,128)(2,1)S(1)}, bf16[128,320]{0,1:T(8,128)(2,1)S(1)}, u32[]{:S(2)}, u32[]{:S(2)}) collective-permute-start(bf16[128,320]{0,1:T(8,128)(2,1)S(1)} %collective-permute-done.11), channel_id=1, source_target_pairs={{0,32},{32,64},{64,96},{96,128},{128,160},{160,192},{192,224},{224... | collective-permute-start | bytes 245768 | tf_op jit(solution)/shard_map/gather_sequence/ppermute | solution.py:30
  100.4 17.0 %collective-permute-start.6 = (bf16[128,320]{0,1:T(8,128)(2,1)S(1)}, bf16[128,320]{0,1:T(8,128)(2,1)S(1)}, u32[]{:S(2)}, u32[]{:S(2)}) collective-permute-start(bf16[128,320]{0,1:T(8,128)(2,1)S(1)} %collective-permute-done.5), channel_id=1, source_target_pairs={{0,480},{32,0},{64,32},{96,64},{128,96},{160,128},{192,160},{224,1... | collective-permute-start | bytes 245768 | tf_op jit(solution)/shard_map/gather_sequence/ppermute | solution.py:30
  106.7 8.8 %collective-permute-start.13 = (bf16[128,320]{0,1:T(8,128)(2,1)S(1)}, bf16[128,320]{0,1:T(8,128)(2,1)S(1)}, u32[]{:S(2)}, u32[]{:S(2)}) collective-permute-start(bf16[128,320]{0,1:T(8,128)(2,1)S(1)} %collective-permute-done.12), channel_id=1, source_target_pairs={{0,32},{32,64},{64,96},{96,128},{128,160},{160,192},{192,224},{224... | collective-permute-start | bytes 245768 | tf_op jit(solution)/shard_map/gather_sequence/ppermute | solution.py:30
  115.5 8.9 %collective-permute-start.14 = (bf16[128,320]{0,1:T(8,128)(2,1)S(1)}, bf16[128,320]{0,1:T(8,128)(2,1)S(1)}, u32[]{:S(2)}, u32[]{:S(2)}) collective-permute-start(bf16[128,320]{0,1:T(8,128)(2,1)S(1)} %collective-permute-done.13), channel_id=1, source_target_pairs={{0,32},{32,64},{64,96},{96,128},{128,160},{160,192},{192,224},{224... | collective-permute-start | bytes 245768 | tf_op jit(solution)/shard_map/gather_sequence/ppermute | solution.py:30
  129.6 25.0 %collective-permute-start.15 = (bf16[2048,320]{0,1:T(8,128)(2,1)}, bf16[2048,320]{0,1:T(8,128)(2,1)}, u32[]{:S(2)}, u32[]{:S(2)}) collective-permute-start(bf16[2048,320]{0,1:T(8,128)(2,1)} %constant_dynamic-update-slice_fusion), channel_id=1, source_target_pairs={{0,8},{8,16},{16,24},{24,0},{1,9},{9,17},{17,25},{25,1},{2,10},{10... | collective-permute-start | bytes 3932168 | tf_op jit(solution)/shard_map/gather_sequence/ppermute | solution.py:30
  133.2 21.5 %collective-permute-start.16 = (bf16[2048,320]{0,1:T(8,128)(2,1)}, bf16[2048,320]{0,1:T(8,128)(2,1)}, u32[]{:S(2)}, u32[]{:S(2)}) collective-permute-start(bf16[2048,320]{0,1:T(8,128)(2,1)} %constant_dynamic-update-slice_fusion), channel_id=1, source_target_pairs={{0,24},{8,0},{16,8},{24,16},{1,25},{9,1},{17,9},{25,17},{2,26},{10... | collective-permute-start | bytes 3932168 | tf_op jit(solution)/shard_map/gather_sequence/ppermute | solution.py:30
  155.3 24.7 %all-to-all-start = ((f32[64,2,2,128]{3,2,1,0:T(2,128)}), f32[64,2,2,128]{3,2,1,0:T(2,128)}, u32[]{:S(2)}, u32[]{:S(2)}) async-start(f32[64,2,2,128]{3,2,1,0:T(2,128)} %broadcast_in_dim.87), calls=%async_computation | async-start | bytes 262144 | tf_op jit(solution)/shard_map/gather_row_stats/all_to_all | solution.py:153
  166.0 24.6 %collective-permute-start.17 = (bf16[1024,320]{0,1:T(8,128)(2,1)}, bf16[1024,320]{0,1:T(8,128)(2,1)}, u32[]{:S(2)}, u32[]{:S(2)}) collective-permute-start(bf16[1024,320]{0,1:T(8,128)(2,1)} %slice.137), channel_id=1, source_target_pairs={{0,8},{8,16},{16,24},{24,0},{1,9},{9,17},{17,25},{25,1},{2,10},{10... | collective-permute-start | bytes 1966088 | tf_op jit(solution)/shard_map/gather_row_stats/ppermute | solution.py:30
  171.4 20.4 %collective-permute-start.18 = (bf16[1024,320]{0,1:T(8,128)(2,1)}, bf16[1024,320]{0,1:T(8,128)(2,1)}, u32[]{:S(2)}, u32[]{:S(2)}) collective-permute-start(bf16[1024,320]{0,1:T(8,128)(2,1)} %slice.138), channel_id=1, source_target_pairs={{0,24},{8,0},{16,8},{24,16},{1,25},{9,1},{17,9},{25,17},{2,26},{10... | collective-permute-start | bytes 1966088 | tf_op jit(solution)/shard_map/gather_row_stats/ppermute | solution.py:30
  (14 other events, 79.8 us)
Sparse Core Ops, SparseCore 0:
  37.1 91.6 all-gather.1
where the time goes:
time: 221 us; the launch traced here: 220 us
  starting transfers between devices  82.2 us (37%)
  blocking collectives  41.9 us (19%)
  local copies, waits for them, and re-layouts  31.9 us (14%)
  matrix products  21.5 us (10%)
  waiting for transfers between devices  19.3 us (9%)
  between operations  14.8 us (7%)
  other arithmetic  7.99 us (4%)
    ppermute x19, starting transfers between devices, shift(): lax.ppermute(data, axis, [(i, (i + step) % size) for i in range(size)])  73.6 us
    ppermute x19, waiting for transfers between devices, shift(): lax.ppermute(data, axis, [(i, (i + step) % size) for i in range(size)])  17.5 us
    all_gather x1, blocking collectives, per_device(): gathered = lax.all_gather(both, 'tp', axis=1, tiled=True)  15.7 us
    all_to_all x1, blocking collectives, per_device(): received = lax.all_to_all(payload, 'tp', 0, 0, tiled=False)  13.8 us
    all_gather x1, blocking collectives, per_device(): kv_all = lax.all_gather(kv, 'y', axis=0, tiled=True)  12.3 us
    unnamed x50, local copies, waits for them, and re-layouts  11.4 us
    all_to_all x1, starting transfers between devices, per_device(): stats_all = lax.all_to_all(sent, ('z', 'y'), 0, 0, tiled=False)  8.64 us
    slice x3, local copies, waits for them, and re-layouts, per_device(): grad_part = piece[:, cols:].reshape(piece_rows, heads_here, head_width)  5.4 us
  transfers between devices with their start and end apart: 21, of which 12 were waited for; matrix products, arithmetic and copies ran while one was open for 23% of the time, Pallas kernels for 0%

commit v1 on v0

--- a/solution.py
+++ b/solution.py
@@ -71,7 +71,24 @@
     contract = (((1,), (1,)), ((), ()))
     with jax.named_scope("gather_features"):
         both = jnp.concatenate([inputs, out_grads], axis=1)
-        gathered = lax.all_gather(both, "tp", axis=1, tiled=True)
+        count, here, width = (lax.axis_size("tp"), lax.axis_index("tp"), both.shape[1])
+        right = [(i_2, (i_2 + 1) % count) for i_2 in range(count)]
+        backward_2 = [(i_2, (i_2 - 1) % count) for i_2 in range(count)]
+        out = jnp.zeros((*both.shape[:1], count * width, *both.shape[1 + 1 :]), both.dtype)
+        out = lax.dynamic_update_slice_in_dim(out, both, here * width, axis=1)
+        from_left = from_right = both
+        middle = count // 2
+        for turn in range(1, middle + 1):
+            from_left = lax.ppermute(from_left, "tp", right)
+            out = lax.dynamic_update_slice_in_dim(
+                out, from_left, (here - turn) % count * width, axis=1
+            )
+            if turn < count - middle:
+                from_right = lax.ppermute(from_right, "tp", backward_2)
+                out = lax.dynamic_update_slice_in_dim(
+                    out, from_right, (here + turn) % count * width, axis=1
+                )
+        gathered = out
         gathered = gathered.reshape(row_count, tp_size, 2, width_here)
         full_inputs = gathered[:, :, 0, :].reshape(row_count, tp_size * width_here)
         full_grads = gathered[:, :, 1, :].reshape(row_count, tp_size * width_here)

time: 221 us -> 229 us (1.036)
  blocking collectives: 41.9 us -> 25.7 us
  waiting for transfers between devices: 19.3 us -> 29.4 us
  starting transfers between devices: 82.2 us -> 92.1 us
    all_gather x1 -> x0, blocking collectives: 15.7 us -> none  [per_device(): gathered = lax.all_gather(both, 'tp', axis=1, tiled=True)]
    ppermute x0 -> x3, starting transfers between devices: none -> 11.6 us  [the longest x1 6.34 us: per_device(): from_right = lax.ppermute(from_right, 'tp', backward_2)]
    ppermute x0 -> x3, waiting for transfers between devices: none -> 8.81 us  [the longest x2 8.8 us: per_device(): from_left = lax.ppermute(from_left, 'tp', right)]
    ppermute x19, starting transfers between devices: 73.6 us -> 70.9 us  [shift(): lax.ppermute(data, axis, [(i, (i + step) % size) for i in range(size)])]
    unnamed x50 -> x47, local copies, waits for them, and re-layouts: 11.4 us -> 12.3 us
  transfers between devices with their start and end apart: 21 -> 24, of which waited for: 12 -> 16; matrix products, arithmetic and copies ran while one was open for 23% -> 23% of each run, Pallas kernels for 0% -> 0%
where the time goes in v1:
time: 229 us; the launch traced here: 227 us
  starting transfers between devices  92.1 us (40%)
  local copies, waits for them, and re-layouts  33.9 us (15%)
  waiting for transfers between devices  29.4 us (13%)
  blocking collectives  25.7 us (11%)
  matrix products  23.6 us (10%)
  between operations  14.9 us (7%)
  other arithmetic  7.74 us (3%)
    ppermute x19, starting transfers between devices, shift(): lax.ppermute(data, axis, [(i, (i + step) % size) for i in range(size)])  70.9 us
    ppermute x19, waiting for transfers between devices, shift(): lax.ppermute(data, axis, [(i, (i + step) % size) for i in range(size)])  18.8 us
    all_to_all x1, blocking collectives, per_device(): received = lax.all_to_all(payload, 'tp', 0, 0, tiled=False)  13.7 us
    unnamed x47, local copies, waits for them, and re-layouts  12.3 us
    all_gather x1, blocking collectives, per_device(): kv_all = lax.all_gather(kv, 'y', axis=0, tiled=True)  12 us
    all_to_all x1, starting transfers between devices, per_device(): stats_all = lax.all_to_all(sent, ('z', 'y'), 0, 0, tiled=False)  9.52 us
    ppermute x2, waiting for transfers between devices, per_device(): from_left = lax.ppermute(from_left, 'tp', right)  8.8 us
    ppermute x1, starting transfers between devices, per_device(): from_right = lax.ppermute(from_right, 'tp', backward_2)  6.34 us
  transfers between devices with their start and end apart: 24, of which 16 were waited for; matrix products, arithmetic and copies ran while one was open for 23% of the time, Pallas kernels for 0%

profile of v1, /device:TPU:2, one launch (start us, length us, event | category | flops | bytes accessed | tf_op | source)
XLA Modules:
  0.0 227.4 jit_solution(14965207491659823071)
XLA Ops:
  8.4 3.4 %collective-permute-start = (bf16[128,640]{0,1:T(8,128)(2,1)S(1)}, bf16[128,640]{0,1:T(8,128)(2,1)S(1)}, u32[]{:S(2)}, u32[]{:S(2)}) collective-permute-start(bf16[128,640]{0,1:T(8,128)(2,1)S(1)} %constant_dynamic-update-slice_fusion), channel_id=1, source_target_pairs={{0,2},{2,4},{4,6},{6,0},{1,3},{3,5},{5,7},{7,1},{8,10},{10,12},{12... | collective-permute-start | bytes 491528 | tf_op jit(solution)/shard_map/gather_features/ppermute | solution.py:82
  11.8 6.3 %collective-permute-start.1 = (bf16[128,640]{0,1:T(8,128)(2,1)S(1)}, bf16[128,640]{0,1:T(8,128)(2,1)S(1)}, u32[]{:S(2)}, u32[]{:S(2)}) collective-permute-start(bf16[128,640]{0,1:T(8,128)(2,1)S(1)} %constant_dynamic-update-slice_fusion), channel_id=1, source_target_pairs={{0,6},{2,0},{4,2},{6,4},{1,7},{3,1},{5,3},{7,5},{8,14},{10,8},{12,... | collective-permute-start | bytes 491528 | tf_op jit(solution)/shard_map/gather_features/ppermute | solution.py:87
  22.2 6.9 %collective-permute-done.2 = bf16[128,640]{0,1:T(8,128)(2,1)S(1)} collective-permute-done((bf16[128,640]{0,1:T(8,128)(2,1)S(1)}, bf16[128,640]{0,1:T(8,128)(2,1)S(1)}, u32[]{:S(2)}, u32[]{:S(2)}) %collective-permute-start.2) | collective-permute-done | bytes 163872 | tf_op jit(solution)/shard_map/gather_features/ppermute | solution.py:82
  31.3 12.0 %all_gather.6 = bf16[512,320]{0,1:T(8,128)(2,1)} all-gather(bf16[128,320]{0,1:T(8,128)(2,1)S(1)} %pad_maximum_fusion.1), channel_id=1, replica_groups=mesh['z'=16,'y'=4,'tp'=4,'dp'=2] {'y'}, dimensions={0}, use_global_device_ids=true | all-gather | bytes 409600 | tf_op jit(solution)/shard_map/gather_sequence/all_gather | solution.py:120
  49.7 7.6 %collective-permute-start.3 = (bf16[128,320]{0,1:T(8,128)(2,1)S(1)}, bf16[128,320]{0,1:T(8,128)(2,1)S(1)}, u32[]{:S(2)}, u32[]{:S(2)}) collective-permute-start(bf16[128,320]{0,1:T(8,128)(2,1)S(1)} %get-tuple-element.59), channel_id=1, source_target_pairs={{0,480},{32,0},{64,32},{96,64},{128,96},{160,128},{192,160},{224,1... | collective-permute-start | bytes 245768 | tf_op jit(solution)/shard_map/gather_sequence/ppermute | solution.py:30
  61.3 5.6 %collective-permute-start.4 = (bf16[128,320]{0,1:T(8,128)(2,1)S(1)}, bf16[128,320]{0,1:T(8,128)(2,1)S(1)}, u32[]{:S(2)}, u32[]{:S(2)}) collective-permute-start(bf16[128,320]{0,1:T(8,128)(2,1)S(1)} %collective-permute-done.3), channel_id=1, source_target_pairs={{0,480},{32,0},{64,32},{96,64},{128,96},{160,128},{192,160},{224,1... | collective-permute-start | bytes 245768 | tf_op jit(solution)/shard_map/gather_sequence/ppermute | solution.py:30
  70.9 5.6 %collective-permute-start.5 = (bf16[128,320]{0,1:T(8,128)(2,1)S(1)}, bf16[128,320]{0,1:T(8,128)(2,1)S(1)}, u32[]{:S(2)}, u32[]{:S(2)}) collective-permute-start(bf16[128,320]{0,1:T(8,128)(2,1)S(1)} %collective-permute-done.4), channel_id=1, source_target_pairs={{0,480},{32,0},{64,32},{96,64},{128,96},{160,128},{192,160},{224,1... | collective-permute-start | bytes 245768 | tf_op jit(solution)/shard_map/gather_sequence/ppermute | solution.py:30
  80.6 5.6 %collective-permute-start.6 = (bf16[128,320]{0,1:T(8,128)(2,1)S(1)}, bf16[128,320]{0,1:T(8,128)(2,1)S(1)}, u32[]{:S(2)}, u32[]{:S(2)}) collective-permute-start(bf16[128,320]{0,1:T(8,128)(2,1)S(1)} %collective-permute-done.5), channel_id=1, source_target_pairs={{0,480},{32,0},{64,32},{96,64},{128,96},{160,128},{192,160},{224,1... | collective-permute-start | bytes 245768 | tf_op jit(solution)/shard_map/gather_sequence/ppermute | solution.py:30
  89.7 5.6 %collective-permute-start.7 = (bf16[128,320]{0,1:T(8,128)(2,1)S(1)}, bf16[128,320]{0,1:T(8,128)(2,1)S(1)}, u32[]{:S(2)}, u32[]{:S(2)}) collective-permute-start(bf16[128,320]{0,1:T(8,128)(2,1)S(1)} %collective-permute-done.6), channel_id=1, source_target_pairs={{0,480},{32,0},{64,32},{96,64},{128,96},{160,128},{192,160},{224,1... | collective-permute-start | bytes 245768 | tf_op jit(solution)/shard_map/gather_sequence/ppermute | solution.py:30
  98.6 5.6 %collective-permute-start.8 = (bf16[128,320]{0,1:T(8,128)(2,1)S(1)}, bf16[128,320]{0,1:T(8,128)(2,1)S(1)}, u32[]{:S(2)}, u32[]{:S(2)}) collective-permute-start(bf16[128,320]{0,1:T(8,128)(2,1)S(1)} %collective-permute-done.7), channel_id=1, source_target_pairs={{0,480},{32,0},{64,32},{96,64},{128,96},{160,128},{192,160},{224,1... | collective-permute-start | bytes 245768 | tf_op jit(solution)/shard_map/gather_sequence/ppermute | solution.py:30
  107.6 5.6 %collective-permute-start.9 = (bf16[128,320]{0,1:T(8,128)(2,1)S(1)}, bf16[128,320]{0,1:T(8,128)(2,1)S(1)}, u32[]{:S(2)}, u32[]{:S(2)}) collective-permute-start(bf16[128,320]{0,1:T(8,128)(2,1)S(1)} %collective-permute-done.8), channel_id=1, source_target_pairs={{0,480},{32,0},{64,32},{96,64},{128,96},{160,128},{192,160},{224,1... | collective-permute-start | bytes 245768 | tf_op jit(solution)/shard_map/gather_sequence/ppermute | solution.py:30
  116.2 6.3 %collective-permute-done.16 = bf16[128,320]{0,1:T(8,128)(2,1)S(1)} collective-permute-done((bf16[128,320]{0,1:T(8,128)(2,1)S(1)}, bf16[128,320]{0,1:T(8,128)(2,1)S(1)}, u32[]{:S(2)}, u32[]{:S(2)}) %collective-permute-start.16) | collective-permute-done | bytes 81952 | tf_op jit(solution)/shard_map/gather_sequence/ppermute | solution.py:30
  125.1 5.4 %collective-permute-done.17 = bf16[128,320]{0,1:T(8,128)(2,1)S(1)} collective-permute-done((bf16[128,320]{0,1:T(8,128)(2,1)S(1)}, bf16[128,320]{0,1:T(8,128)(2,1)S(1)}, u32[]{:S(2)}, u32[]{:S(2)}) %collective-permute-start.17) | collective-permute-done | bytes 81952 | tf_op jit(solution)/shard_map/gather_sequence/ppermute | solution.py:30
  135.7 2.5 %collective-permute-start.18 = (bf16[2048,320]{0,1:T(8,128)(2,1)}, bf16[2048,320]{0,1:T(8,128)(2,1)}, u32[]{:S(2)}, u32[]{:S(2)}) collective-permute-start(bf16[2048,320]{0,1:T(8,128)(2,1)} %constant_dynamic-update-slice_fusion.2), channel_id=1, source_target_pairs={{0,8},{8,16},{16,24},{24,0},{1,9},{9,17},{17,25},{25,1},{2,10},{10... | collective-permute-start | bytes 3932168 | tf_op jit(solution)/shard_map/gather_sequence/ppermute | solution.py:30
  138.2 4.8 %collective-permute-start.19 = (bf16[2048,320]{0,1:T(8,128)(2,1)}, bf16[2048,320]{0,1:T(8,128)(2,1)}, u32[]{:S(2)}, u32[]{:S(2)}) collective-permute-start(bf16[2048,320]{0,1:T(8,128)(2,1)} %constant_dynamic-update-slice_fusion.2), channel_id=1, source_target_pairs={{0,24},{8,0},{16,8},{24,16},{1,25},{9,1},{17,9},{25,17},{2,26},{10... | collective-permute-start | bytes 3932168 | tf_op jit(solution)/shard_map/gather_sequence/ppermute | solution.py:30
  145.2 3.0 %fusion.51 = (bf16[8192,160]{0,1:T(8,128)(2,1)S(1)}, bf16[8192,160]{0,1:T(8,128)(2,1)S(1)}) fusion(bf16[8192,320]{0,1:T(8,128)(2,1)} %all-gather.2.cloned.1.call-done), kind=kLoop, calls=%fused_computation.133 | loop fusion | bytes 10485760 | tf_op jit(solution)/shard_map/gather_sequence/slice | solution.py:125
  150.0 2.5 %select_reduce_fusion = f32[2,128]{1,0:T(2,128)S(1)} fusion(f32[2,128,8192]{2,1,0:T(8,128)S(1)} %get-tuple-element.70, f32[2,128]{1,0:T(2,128)S(1)} %get-tuple-element.69, pred[128,8192]{1,0:T(8,128)(4,1)S(1)} %broadcast_compare_fusion), kind=kLoop, calls=%fused_computation.4 | loop fusion | flops 8388352 | bytes 9439232 | tf_op jit(solution)/shard_map/query_pass/reduce_sum | solution.py:145
  152.5 3.5 %fusion.57 = (f32[2,128]{1,0:T(2,128)S(1)}, bf16[2,128,8192]{2,1,0:T(8,128)(2,1)S(1)}) fusion(bf16[128,2,80]{0,2,1:T(8,128)(2,1)S(1)} %bitcast.192, bf16[8192,2,80]{0,2,1:T(8,128)(2,1)S(1)} %bitcast.178, f32[2,128,8192]{2,1,0:T(8,128)S(1)} %get-tuple-element.70, f32[2,128]{1,0:T(2,128)S(1)} %log_add_fusion, pred[128,8192]{1,0:T(8,128)(4,1)S(1)} %broadcast_compare_fusion), kind=kOutput, calls=%fused_computation.139 | convolution fusion | flops 346029824 | bytes 16295936 | tf_op jit(solution)/shard_map/query_pass/qhd,khd->hqk/dot_general | solution.py:148
  162.3 9.5 %all-to-all-start = ((f32[64,2,2,128]{3,2,1,0:T(2,128)}), f32[64,2,2,128]{3,2,1,0:T(2,128)}, u32[]{:S(2)}, u32[]{:S(2)}) async-start(f32[64,2,2,128]{3,2,1,0:T(2,128)} %broadcast_in_dim.91), calls=%async_computation | async-start | bytes 262144 | tf_op jit(solution)/shard_map/gather_row_stats/all_to_all | solution.py:170
  173.8 3.4 %collective-permute-start.20 = (bf16[1024,320]{0,1:T(8,128)(2,1)}, bf16[1024,320]{0,1:T(8,128)(2,1)}, u32[]{:S(2)}, u32[]{:S(2)}) collective-permute-start(bf16[1024,320]{0,1:T(8,128)(2,1)} %slice.137), channel_id=1, source_target_pairs={{0,8},{8,16},{16,24},{24,0},{1,9},{9,17},{17,25},{25,1},{2,10},{10... | collective-permute-start | bytes 1966088 | tf_op jit(solution)/shard_map/gather_row_stats/ppermute | solution.py:30
  179.2 3.9 %collective-permute-start.21 = (bf16[1024,320]{0,1:T(8,128)(2,1)}, bf16[1024,320]{0,1:T(8,128)(2,1)}, u32[]{:S(2)}, u32[]{:S(2)}) collective-permute-start(bf16[1024,320]{0,1:T(8,128)(2,1)} %slice.138), channel_id=1, source_target_pairs={{0,24},{8,0},{16,8},{24,16},{1,25},{9,1},{17,9},{25,17},{2,26},{10... | collective-permute-start | bytes 1966088 | tf_op jit(solution)/shard_map/gather_row_stats/ppermute | solution.py:30
  183.1 3.0 %fusion.53 = (bf16[2048,160]{0,1:T(8,128)(2,1)}, bf16[2048,160]{0,1:T(8,128)(2,1)S(1)}, bf16[2048,160]{0,1:T(8,128)(2,1)S(1)}, bf16[2048,160]{0,1:T(8,128)(2,1)}) fusion(bf16[2048,320]{0,1:T(8,128)(2,1)} %collective-permute-done.19, bf16[2048,320]{0,1:T(8,128)(2,1)} %collective-permute-done.18), kind=kLoop, calls=%fused_computation.135 | loop fusion | bytes 5242880 | tf_op jit(solution)/shard_map/key_pass/slice | solution.py:180
  187.9 2.3 gather_fusion.1
  205.9 13.7 %all_to_all.10 = f32[4,129,320]{2,1,0:T(8,128)S(1)} all-to-all(f32[4,129,320]{2,1,0:T(8,128)S(1)} %copy.27), channel_id=1, replica_groups=mesh['z'=16,'y'=4,'tp'=4,'dp'=2] {'tp'}, dimensions={0} | all-to-all | bytes 1320960 | tf_op jit(solution)/shard_map/back_projection/all_to_all | solution.py:214
  (157 shorter events, 79.1 us)
Async XLA Ops:
  6.5 138.6 %all-gather.2.cloned.1.call-start = ((), (), s32[]{:S(2)}) async-start(), calls=%async_computation.2 | async-start | bytes 5570560 | tf_op jit(solution)/shard_map/gather_sequence/all_gather | solution.py:121
  8.4 11.8 %collective-permute-start = (bf16[128,640]{0,1:T(8,128)(2,1)S(1)}, bf16[128,640]{0,1:T(8,128)(2,1)S(1)}, u32[]{:S(2)}, u32[]{:S(2)}) collective-permute-start(bf16[128,640]{0,1:T(8,128)(2,1)S(1)} %constant_dynamic-update-slice_fusion), channel_id=1, source_target_pairs={{0,2},{2,4},{4,6},{6,0},{1,3},{3,5},{5,7},{7,1},{8,10},{10,12},{12... | collective-permute-start | bytes 491528 | tf_op jit(solution)/shard_map/gather_features/ppermute | solution.py:82
  11.8 10.4 %collective-permute-start.1 = (bf16[128,640]{0,1:T(8,128)(2,1)S(1)}, bf16[128,640]{0,1:T(8,128)(2,1)S(1)}, u32[]{:S(2)}, u32[]{:S(2)}) collective-permute-start(bf16[128,640]{0,1:T(8,128)(2,1)S(1)} %constant_dynamic-update-slice_fusion), channel_id=1, source_target_pairs={{0,6},{2,0},{4,2},{6,4},{1,7},{3,1},{5,3},{7,5},{8,14},{10,8},{12,... | collective-permute-start | bytes 491528 | tf_op jit(solution)/shard_map/gather_features/ppermute | solution.py:87
  20.2 8.9 %collective-permute-start.2 = (bf16[128,640]{0,1:T(8,128)(2,1)S(1)}, bf16[128,640]{0,1:T(8,128)(2,1)S(1)}, u32[]{:S(2)}, u32[]{:S(2)}) collective-permute-start(bf16[128,640]{0,1:T(8,128)(2,1)S(1)} %collective-permute-done), channel_id=1, source_target_pairs={{0,2},{2,4},{4,6},{6,0},{1,3},{3,5},{5,7},{7,1},{8,10},{10,12},{12... | collective-permute-start | bytes 491528 | tf_op jit(solution)/shard_map/gather_features/ppermute | solution.py:82
  49.7 11.5 %collective-permute-start.3 = (bf16[128,320]{0,1:T(8,128)(2,1)S(1)}, bf16[128,320]{0,1:T(8,128)(2,1)S(1)}, u32[]{:S(2)}, u32[]{:S(2)}) collective-permute-start(bf16[128,320]{0,1:T(8,128)(2,1)S(1)} %get-tuple-element.59), channel_id=1, source_target_pairs={{0,480},{32,0},{64,32},{96,64},{128,96},{160,128},{192,160},{224,1... | collective-permute-start | bytes 245768 | tf_op jit(solution)/shard_map/gather_sequence/ppermute | solution.py:30
  57.4 9.5 %collective-permute-start.10 = (bf16[128,320]{0,1:T(8,128)(2,1)S(1)}, bf16[128,320]{0,1:T(8,128)(2,1)S(1)}, u32[]{:S(2)}, u32[]{:S(2)}) collective-permute-start(bf16[128,320]{0,1:T(8,128)(2,1)S(1)} %get-tuple-element.59), channel_id=1, source_target_pairs={{0,32},{32,64},{64,96},{96,128},{128,160},{160,192},{192,224},{224... | collective-permute-start | bytes 245768 | tf_op jit(solution)/shard_map/gather_sequence/ppermute | solution.py:30
  61.3 9.6 %collective-permute-start.4 = (bf16[128,320]{0,1:T(8,128)(2,1)S(1)}, bf16[128,320]{0,1:T(8,128)(2,1)S(1)}, u32[]{:S(2)}, u32[]{:S(2)}) collective-permute-start(bf16[128,320]{0,1:T(8,128)(2,1)S(1)} %collective-permute-done.3), channel_id=1, source_target_pairs={{0,480},{32,0},{64,32},{96,64},{128,96},{160,128},{192,160},{224,1... | collective-permute-start | bytes 245768 | tf_op jit(solution)/shard_map/gather_sequence/ppermute | solution.py:30
  66.9 9.9 %collective-permute-start.11 = (bf16[128,320]{0,1:T(8,128)(2,1)S(1)}, bf16[128,320]{0,1:T(8,128)(2,1)S(1)}, u32[]{:S(2)}, u32[]{:S(2)}) collective-permute-start(bf16[128,320]{0,1:T(8,128)(2,1)S(1)} %collective-permute-done.10), channel_id=1, source_target_pairs={{0,32},{32,64},{64,96},{96,128},{128,160},{160,192},{192,224},{224... | collective-permute-start | bytes 245768 | tf_op jit(solution)/shard_map/gather_sequence/ppermute | solution.py:30
  70.9 9.7 %collective-permute-start.5 = (bf16[128,320]{0,1:T(8,128)(2,1)S(1)}, bf16[128,320]{0,1:T(8,128)(2,1)S(1)}, u32[]{:S(2)}, u32[]{:S(2)}) collective-permute-start(bf16[128,320]{0,1:T(8,128)(2,1)S(1)} %collective-permute-done.4), channel_id=1, source_target_pairs={{0,480},{32,0},{64,32},{96,64},{128,96},{160,128},{192,160},{224,1... | collective-permute-start | bytes 245768 | tf_op jit(solution)/shard_map/gather_sequence/ppermute | solution.py:30
  76.8 9.4 %collective-permute-start.12 = (bf16[128,320]{0,1:T(8,128)(2,1)S(1)}, bf16[128,320]{0,1:T(8,128)(2,1)S(1)}, u32[]{:S(2)}, u32[]{:S(2)}) collective-permute-start(bf16[128,320]{0,1:T(8,128)(2,1)S(1)} %collective-permute-done.11), channel_id=1, source_target_pairs={{0,32},{32,64},{64,96},{96,128},{128,160},{160,192},{192,224},{224... | collective-permute-start | bytes 245768 | tf_op jit(solution)/shard_map/gather_sequence/ppermute | solution.py:30
  80.6 9.1 %collective-permute-start.6 = (bf16[128,320]{0,1:T(8,128)(2,1)S(1)}, bf16[128,320]{0,1:T(8,128)(2,1)S(1)}, u32[]{:S(2)}, u32[]{:S(2)}) collective-permute-start(bf16[128,320]{0,1:T(8,128)(2,1)S(1)} %collective-permute-done.5), channel_id=1, source_target_pairs={{0,480},{32,0},{64,32},{96,64},{128,96},{160,128},{192,160},{224,1... | collective-permute-start | bytes 245768 | tf_op jit(solution)/shard_map/gather_sequence/ppermute | solution.py:30
  86.2 9.2 %collective-permute-start.13 = (bf16[128,320]{0,1:T(8,128)(2,1)S(1)}, bf16[128,320]{0,1:T(8,128)(2,1)S(1)}, u32[]{:S(2)}, u32[]{:S(2)}) collective-permute-start(bf16[128,320]{0,1:T(8,128)(2,1)S(1)} %collective-permute-done.12), channel_id=1, source_target_pairs={{0,32},{32,64},{64,96},{96,128},{128,160},{160,192},{192,224},{224... | collective-permute-start | bytes 245768 | tf_op jit(solution)/shard_map/gather_sequence/ppermute | solution.py:30
  89.7 8.9 %collective-permute-start.7 = (bf16[128,320]{0,1:T(8,128)(2,1)S(1)}, bf16[128,320]{0,1:T(8,128)(2,1)S(1)}, u32[]{:S(2)}, u32[]{:S(2)}) collective-permute-start(bf16[128,320]{0,1:T(8,128)(2,1)S(1)} %collective-permute-done.6), channel_id=1, source_target_pairs={{0,480},{32,0},{64,32},{96,64},{128,96},{160,128},{192,160},{224,1... | collective-permute-start | bytes 245768 | tf_op jit(solution)/shard_map/gather_sequence/ppermute | solution.py:30
  95.4 9.1 %collective-permute-start.14 = (bf16[128,320]{0,1:T(8,128)(2,1)S(1)}, bf16[128,320]{0,1:T(8,128)(2,1)S(1)}, u32[]{:S(2)}, u32[]{:S(2)}) collective-permute-start(bf16[128,320]{0,1:T(8,128)(2,1)S(1)} %collective-permute-done.13), channel_id=1, source_target_pairs={{0,32},{32,64},{64,96},{96,128},{128,160},{160,192},{192,224},{224... | collective-permute-start | bytes 245768 | tf_op jit(solution)/shard_map/gather_sequence/ppermute | solution.py:30
  98.6 9.0 %collective-permute-start.8 = (bf16[128,320]{0,1:T(8,128)(2,1)S(1)}, bf16[128,320]{0,1:T(8,128)(2,1)S(1)}, u32[]{:S(2)}, u32[]{:S(2)}) collective-permute-start(bf16[128,320]{0,1:T(8,128)(2,1)S(1)} %collective-permute-done.7), channel_id=1, source_target_pairs={{0,480},{32,0},{64,32},{96,64},{128,96},{160,128},{192,160},{224,1... | collective-permute-start | bytes 245768 | tf_op jit(solution)/shard_map/gather_sequence/ppermute | solution.py:30
  104.5 9.0 %collective-permute-start.15 = (bf16[128,320]{0,1:T(8,128)(2,1)S(1)}, bf16[128,320]{0,1:T(8,128)(2,1)S(1)}, u32[]{:S(2)}, u32[]{:S(2)}) collective-permute-start(bf16[128,320]{0,1:T(8,128)(2,1)S(1)} %collective-permute-done.14), channel_id=1, source_target_pairs={{0,32},{32,64},{64,96},{96,128},{128,160},{160,192},{192,224},{224... | collective-permute-start | bytes 245768 | tf_op jit(solution)/shard_map/gather_sequence/ppermute | solution.py:30
  107.6 16.8 %collective-permute-start.9 = (bf16[128,320]{0,1:T(8,128)(2,1)S(1)}, bf16[128,320]{0,1:T(8,128)(2,1)S(1)}, u32[]{:S(2)}, u32[]{:S(2)}) collective-permute-start(bf16[128,320]{0,1:T(8,128)(2,1)S(1)} %collective-permute-done.8), channel_id=1, source_target_pairs={{0,480},{32,0},{64,32},{96,64},{128,96},{160,128},{192,160},{224,1... | collective-permute-start | bytes 245768 | tf_op jit(solution)/shard_map/gather_sequence/ppermute | solution.py:30
  113.6 8.9 %collective-permute-start.16 = (bf16[128,320]{0,1:T(8,128)(2,1)S(1)}, bf16[128,320]{0,1:T(8,128)(2,1)S(1)}, u32[]{:S(2)}, u32[]{:S(2)}) collective-permute-start(bf16[128,320]{0,1:T(8,128)(2,1)S(1)} %collective-permute-done.15), channel_id=1, source_target_pairs={{0,32},{32,64},{64,96},{96,128},{128,160},{160,192},{192,224},{224... | collective-permute-start | bytes 245768 | tf_op jit(solution)/shard_map/gather_sequence/ppermute | solution.py:30
  122.5 7.9 %collective-permute-start.17 = (bf16[128,320]{0,1:T(8,128)(2,1)S(1)}, bf16[128,320]{0,1:T(8,128)(2,1)S(1)}, u32[]{:S(2)}, u32[]{:S(2)}) collective-permute-start(bf16[128,320]{0,1:T(8,128)(2,1)S(1)} %collective-permute-done.16), channel_id=1, source_target_pairs={{0,32},{32,64},{64,96},{96,128},{128,160},{160,192},{192,224},{224... | collective-permute-start | bytes 245768 | tf_op jit(solution)/shard_map/gather_sequence/ppermute | solution.py:30
  135.7 25.0 %collective-permute-start.18 = (bf16[2048,320]{0,1:T(8,128)(2,1)}, bf16[2048,320]{0,1:T(8,128)(2,1)}, u32[]{:S(2)}, u32[]{:S(2)}) collective-permute-start(bf16[2048,320]{0,1:T(8,128)(2,1)} %constant_dynamic-update-slice_fusion.2), channel_id=1, source_target_pairs={{0,8},{8,16},{16,24},{24,0},{1,9},{9,17},{17,25},{25,1},{2,10},{10... | collective-permute-start | bytes 3932168 | tf_op jit(solution)/shard_map/gather_sequence/ppermute | solution.py:30
  138.2 23.5 %collective-permute-start.19 = (bf16[2048,320]{0,1:T(8,128)(2,1)}, bf16[2048,320]{0,1:T(8,128)(2,1)}, u32[]{:S(2)}, u32[]{:S(2)}) collective-permute-start(bf16[2048,320]{0,1:T(8,128)(2,1)} %constant_dynamic-update-slice_fusion.2), channel_id=1, source_target_pairs={{0,24},{8,0},{16,8},{24,16},{1,25},{9,1},{17,9},{25,17},{2,26},{10... | collective-permute-start | bytes 3932168 | tf_op jit(solution)/shard_map/gather_sequence/ppermute | solution.py:30
  162.3 25.6 %all-to-all-start = ((f32[64,2,2,128]{3,2,1,0:T(2,128)}), f32[64,2,2,128]{3,2,1,0:T(2,128)}, u32[]{:S(2)}, u32[]{:S(2)}) async-start(f32[64,2,2,128]{3,2,1,0:T(2,128)} %broadcast_in_dim.91), calls=%async_computation | async-start | bytes 262144 | tf_op jit(solution)/shard_map/gather_row_stats/all_to_all | solution.py:170
  173.8 24.6 %collective-permute-start.20 = (bf16[1024,320]{0,1:T(8,128)(2,1)}, bf16[1024,320]{0,1:T(8,128)(2,1)}, u32[]{:S(2)}, u32[]{:S(2)}) collective-permute-start(bf16[1024,320]{0,1:T(8,128)(2,1)} %slice.137), channel_id=1, source_target_pairs={{0,8},{8,16},{16,24},{24,0},{1,9},{9,17},{17,25},{25,1},{2,10},{10... | collective-permute-start | bytes 1966088 | tf_op jit(solution)/shard_map/gather_row_stats/ppermute | solution.py:30
  179.2 20.4 %collective-permute-start.21 = (bf16[1024,320]{0,1:T(8,128)(2,1)}, bf16[1024,320]{0,1:T(8,128)(2,1)}, u32[]{:S(2)}, u32[]{:S(2)}) collective-permute-start(bf16[1024,320]{0,1:T(8,128)(2,1)} %slice.138), channel_id=1, source_target_pairs={{0,24},{8,0},{16,8},{24,16},{1,25},{9,1},{17,9},{25,17},{2,26},{10... | collective-permute-start | bytes 1966088 | tf_op jit(solution)/shard_map/gather_row_stats/ppermute | solution.py:30
  (15 other events, 101.7 us)
Sparse Core Ops, SparseCore 0:
  43.4 89.8 all-gather.1
